TPU v7x, 128 devices: a whole 4x4x4 slice. The times are simulated.
128 devices in a mesh: chaos: 8 (over x, y_hi), space: 16 (over y_lo, z, core).
Axes of the slice: x: 4, y: 4 (y_hi: 2, y_lo: 2; y = y_hi * 2 + y_lo), z: 4, core: 2. Of those that a mesh axis runs over, the one named last changes fastest.
Arguments:
- modes: float32 [120, 128, 2048], P('chaos', 'space'), may hold values from -2 to 2
- kl_fields: float32 [8, 128, 2048], P(None, 'space'), may hold values from 0.1 to 1
- triples: int32 [624, 3], replicated, may hold values from 0 to 119, as said below
- ratios: int32 [624, 2], replicated, may hold values from 1 to 12, as said below
- mode_of_slot: int32 [120], replicated, may hold values from 0 to 119, each once
Outputs:
- applied: float32 [120, 128, 2048], P('chaos', 'space')
Inputs may be any that keep to these rules, and one draw needn't show every extreme that they name: `triples`: rows are distinct. Modes are the multi-indices of total degree at most 3 in 7 variables. Every mode i has the row (i, i, 0); every other row (i, j, k) has k of 1 or more, and the multi-indices of i and j differ by one in variable k and agree elsewhere; each such pair appears in both orders. `ratios`: column 0 is a positive numerator, column 1 a denominator of 1 to 4. `mode_of_slot`: A permutation.
All inputs are finite; a program needn't handle non-finite values.
Results may differ from a plain program's by a relative error of at most 0.000082.
Values sent between devices are 32-bit elements; how exact they have to be, the bound alone decides.
No kernel may reach another device: no remote copies, remote signals or barrier semaphores. Data moves between devices by JAX's collectives and lax.ppermute only.
A program may use at most 128 MiB of HBM per device.

v0:
```python
import jax
import jax.numpy as jnp
from jax import lax
from jax.sharding import PartitionSpec as P


def extended_2(x, sides, width):
    for axis, dim in sides:
        count, length = (lax.axis_size(axis), x.shape[dim])
        up = [(i, (i + 1) % count) for i in range(count - 1)]
        down = [(j, i) for i, j in up]
        last = lax.slice_in_dim(x, length - width, length, axis=dim)
        first = lax.slice_in_dim(x, 0, width, axis=dim)
        before = lax.ppermute(last, axis, up)
        after = lax.ppermute(first, axis, down)
        x = jnp.concatenate([before, x, after], axis=dim)
    return x


def shift_cols(x, direction):
    zero = jnp.zeros_like(x[..., :1])
    if direction > 0:
        return jnp.concatenate([zero, x[..., :-1]], axis=-1)
    return jnp.concatenate([x[..., 1:], zero], axis=-1)


def coupling_table(triples, ratios, mode_of_slot, kl_terms, mode_count):
    matches = triples[:, :2, None] == mode_of_slot[None, None, :]
    slot_pairs = jnp.sum(jnp.where(matches, jnp.arange(mode_count, dtype=jnp.int32), 0), axis=2)
    weights = ratios[:, 0].astype(jnp.float32) / ratios[:, 1].astype(jnp.float32)
    flat_index = (triples[:, 2] * mode_count + slot_pairs[:, 0]) * mode_count + slot_pairs[:, 1]
    coupling = (
        jnp.zeros((kl_terms * mode_count * mode_count,), jnp.float32).at[flat_index].add(weights)
    )
    return coupling.reshape(kl_terms, mode_count, mode_count)


def neighbour_table(local_rows):
    mode_count = local_rows.shape[-1]
    present = local_rows > 0
    first = jnp.argmax(present, axis=-1).astype(jnp.int32)
    last = (mode_count - 1 - jnp.argmax(present[..., ::-1], axis=-1)).astype(jnp.int32)
    w_first = jnp.take_along_axis(local_rows, first[..., None], axis=-1)[..., 0]
    w_last = jnp.take_along_axis(local_rows, last[..., None], axis=-1)[..., 0]
    w_last = jnp.where(last == first, jnp.zeros_like(w_last), w_last)
    return (first, last, w_first, w_last)


def local(modes, kl_fields, triples, ratios, mode_of_slot):
    groups = lax.axis_size("chaos")
    own_modes = modes.shape[0]
    mode_count = own_modes * groups
    kl_terms = kl_fields.shape[0]
    first_slot = lax.axis_index("chaos") * own_modes
    coupling = coupling_table(triples, ratios, mode_of_slot, kl_terms, mode_count)
    local_rows = lax.dynamic_slice_in_dim(coupling, first_slot, own_modes, 1)
    first, last, w_first, w_last = neighbour_table(local_rows)
    joined = jnp.concatenate([modes, kl_fields], axis=0)
    padded = extended_2(joined, (("space", 1),), 1)
    source = padded[:own_modes]
    coef = padded[own_modes:]
    every = lax.all_gather(source, "chaos", axis=0, tiled=True)
    a_c = coef[:, 1:-1]
    c_up = (a_c + coef[:, :-2])[:, None]
    c_dn = (a_c + coef[:, 2:])[:, None]
    c_lf = (a_c + shift_cols(a_c, 1))[:, None]
    c_rt = (a_c + shift_cols(a_c, -1))[:, None]
    g_first = jnp.take(every, first.reshape(-1), axis=0).reshape(
        (kl_terms, own_modes) + every.shape[1:]
    )
    g_last = jnp.take(every, last.reshape(-1), axis=0).reshape(
        (kl_terms, own_modes) + every.shape[1:]
    )
    mixed = w_first[:, :, None, None] * g_first + w_last[:, :, None, None] * g_last
    center = mixed[:, :, 1:-1]
    result = c_up * (center - mixed[:, :, :-2])
    result = result + c_dn * (center - mixed[:, :, 2:])
    result = result + c_lf * (center - shift_cols(center, 1))
    result = result + c_rt * (center - shift_cols(center, -1))
    return 0.5 * jnp.sum(result, axis=0)


def solution(mesh):
    return jax.shard_map(
        local,
        mesh=mesh,
        in_specs=(P("chaos", "space", None), P(None, "space", None), P(), P(), P()),
        out_specs=P("chaos", "space", None),
        check_vma=False,
    )
```

profile of v0, /device:TPU:0, one launch (start us, length us, event | category | flops | bytes accessed | tf_op | source)
XLA Modules:
  0.0 301.7 jit_solution(17905389642816986577)
XLA Ops:
  6.6 1.8 copy.16
  8.4 1.4 copy.18
  9.8 1.3 collective-permute-start
  11.1 1.3 collective-permute-start.1
  12.4 4.3 %collective-permute-done.1 = f32[23,1,2048]{2,0,1:T(8,128)S(1)} collective-permute-done((f32[23,1,2048]{2,0,1:T(8,128)S(1)}, f32[23,1,2048]{2,0,1:T(8,128)S(1)}, u32[]{:S(2)}, u32[]{:S(2)}) %collective-permute-start.1) | collective-permute-done | bytes 188448 | tf_op jit(solution)/shard_map/ppermute | solution.py:15
  16.7 0.1 pad_maximum_fusion
  16.8 2.0 copy.20
  18.9 0.1 select_reduce_fusion
  19.1 4.7 %scatter_custom_fusion = f32[115200]{0:T(1024)S(1)} fusion(s32[624]{0:T(1024)S(1)} %fusion.22, f32[624]{0:T(1024)S(1)} %fusion.24, f32[]{:T(128)} %constant.6.clone.1), kind=kCustom, calls=%fused_computation.29 | custom fusion | flops 624 | bytes 460804 | tf_op jit(solution)/shard_map/scatter-add | solution.py:33
  23.8 0.5 reshape.47
  24.4 0.1 rev.3
  24.5 1.1 iota_reduce_fusion.1
  25.7 0.9 iota_reduce_fusion
  26.7 2.1 gather_fusion.2
  28.9 0.1 reshape.99
  28.9 2.1 gather_fusion
  31.1 0.1 reshape.50
  31.3 0.2 fusion.26
  31.5 1.0 pad_add_fusion.1
  32.4 0.1 fusion.7
  32.6 1.1 copy.19
  33.7 1.1 copy.22
  34.8 166.2 %all-gather.2.cloned.1.call-done = f32[120,10,2048]{2,1,0:T(8,128)} async-done(((f32[15,10,2048]{2,1,0:T(8,128)}), f32[120,10,2048]{2,1,0:T(8,128)}) %all-gather.2.cloned.1.call-update) | async-done | bytes 9830416 | tf_op jit(solution)/shard_map/all_gather | solution.py:62
  201.0 15.0 %gather_fusion.1 = f32[120,10,2048]{2,1,0:T(8,128)} fusion(f32[120,10,2048]{2,1,0:T(8,128)} %all-gather.2.cloned.1.call-done, s32[1024]{0:T(1024)S(1)} %pad_clamp_fusion.1), kind=kCustom, calls=%fused_computation.1.clone | custom fusion | bytes 19661280 | tf_op jit(solution)/shard_map/jit(_take)/gather | solution.py:68
  216.0 11.6 %broadcast_select_fusion.1 = f32[120,10,2048]{2,1,0:T(8,128)} fusion(f32[120,10,2048]{2,1,0:T(8,128)} %gather_fusion.1, pred[120]{0:T(512)(128)(4,1)S(1)} %compare_and_fusion.1), kind=kLoop, calls=%fused_computation.15 | loop fusion | flops 2457600 | bytes 19660920 | tf_op jit(solution)/shard_map/jit(_take)/select_n | solution.py:68
  227.7 15.0 %gather_fusion.3 = f32[120,10,2048]{2,1,0:T(8,128)} fusion(f32[120,10,2048]{2,1,0:T(8,128)} %all-gather.2.cloned.1.call-done, s32[1024]{0:T(1024)S(1)} %pad_clamp_fusion), kind=kCustom, calls=%fused_computation.3.clone | custom fusion | bytes 19661280 | tf_op jit(solution)/shard_map/jit(_take)/gather | solution.py:71
  242.7 6.8 %broadcast_select_fusion = f32[120,10,2048]{2,1,0:T(8,128)S(1)} fusion(f32[120,10,2048]{2,1,0:T(8,128)} %gather_fusion.3, pred[120]{0:T(512)(128)(4,1)S(1)} %compare_and_fusion), kind=kLoop, calls=%fused_computation.14 | loop fusion | flops 2457600 | bytes 19660920 | tf_op jit(solution)/shard_map/jit(_take)/select_n | solution.py:71
  249.6 3.2 %copy-done = f32[120,10,2048]{2,1,0:T(8,128)S(1)} copy-done((f32[120,10,2048]{2,1,0:T(8,128)S(1)}, f32[120,10,2048]{2,1,0:T(8,128)}, u32[]{:S(2)}) %copy-start) | copy-done | bytes 9830424
  252.7 7.1 %multiply_add_fusion = f32[8,15,10,2048]{3,2,1,0:T(8,128)} fusion(f32[8,15,10,2048]{3,2,1,0:T(8,128)S(1)} %bitcast.31, f32[8,15,10,2048]{3,2,1,0:T(8,128)S(1)} %bitcast.30, f32[8,15]{1,0:T(8,128)S(1)} %bitcast_select_fusion, f32[8,15]{1,0:T(8,128)S(1)} %select_bitcast_fusion), kind=kLoop, calls=%fused_computation.5 | loop fusion | flops 7372800 | bytes 29492160 | tf_op jit(solution)/shard_map/add | solution.py:74
  259.8 15.7 %fusion.25 = (f32[8,15,8,2047]{3,2,1,0:T(8,128)S(1)}, f32[8,15,8,2047]{3,2,1,0:T(8,128)}) fusion(f32[8,15,10,2048]{3,2,1,0:T(8,128)} %multiply_add_fusion), kind=kLoop, calls=%fused_computation.76 | loop fusion | bytes 31441920 | tf_op jit(solution)/shard_map/slice | solution.py:23
  275.5 18.3 %fusion.4 = f32[15,8,2048]{2,1,0:T(8,128)S(1)} fusion(f32[8,15,10,2048]{3,2,1,0:T(8,128)} %multiply_add_fusion, f32[8,15,8,2047]{3,2,1,0:T(8,128)} %get-tuple-element.14, f32[8,15,8,2047]{3,2,1,0:T(8,128)S(1)} %get-tuple-element.13, f32[8,8,2048]{2,1,0:T(8,128)} %get-tuple-element.20, f32[8,8,2048]{2,1,0:T(8,128)S(1)} %get-tuple-element.19, ...), kind=kLoop, calls=%fused_computation.11 | loop fusion | flops 23347200 | bytes 42394112 | tf_op jit(solution)/shard_map/reduce_sum | solution.py:80
  293.8 1.1 broadcast_multiply_fusion
  (41 shorter events, 0.6 us)
Async XLA Ops:
  6.5 12.3 %slice-start = ((s32[624,3]{0,1:T(4,128)}), s32[624,2]{0,1:T(2,128)S(1)}, s32[]{:S(2)}) async-start(s32[624,3]{0,1:T(4,128)} %param.11), calls=%async_computation.1 | async-start | bytes 10240 | tf_op jit(solution)/shard_map/slice | solution.py:28
  6.5 12.5 %copy-start.4 = (s32[624,3]{0,1:T(4,128)S(1)}, s32[624,3]{0,1:T(4,128)}, u32[]{:S(2)}) copy-start(s32[624,3]{0,1:T(4,128)} %param.11) | copy-start | bytes 22468
  6.5 12.3 %copy-start.6 = (s32[120]{0:T(128)S(1)}, s32[120]{0:T(128)}, u32[]{:S(2)}) copy-start(s32[120]{0:T(128)} %param.13) | copy-start | bytes 1444
  6.5 12.5 %copy-start.5 = (s32[624,2]{0,1:T(2,128)S(1)}, s32[624,2]{0,1:T(2,128)}, u32[]{:S(2)}) copy-start(s32[624,2]{0,1:T(2,128)} %param.12) | copy-start | bytes 14980
  6.5 194.5 %all-gather.2.cloned.1.call-start = ((), (), s32[]{:S(2)}) async-start(), calls=%async_computation | async-start | bytes 17694720 | tf_op jit(solution)/shard_map/all_gather | solution.py:62
  9.8 2.6 collective-permute-start
  11.1 5.6 %collective-permute-start.1 = (f32[23,1,2048]{2,0,1:T(8,128)S(1)}, f32[23,1,2048]{2,0,1:T(8,128)S(1)}, u32[]{:S(2)}, u32[]{:S(2)}) collective-permute-start(f32[23,1,2048]{2,0,1:T(8,128)S(1)} %get-tuple-element.18), channel_id=1, source_target_pairs={{1,0},{2,1},{3,2},{4,3},{5,4},{6,5},{7,6},{8,7},{9,8},{10,9},{11,1... | collective-permute-start | bytes 565256 | tf_op jit(solution)/shard_map/ppermute | solution.py:15
  16.7 2.4 copy-start.2
  16.8 14.5 %copy-start.1 = (f32[8,8,2048]{2,1,0:T(8,128)S(1)}, f32[8,8,2048]{2,1,0:T(8,128)}, u32[]{:S(2)}) copy-start(f32[8,8,2048]{2,1,0:T(8,128)} %param.10) | copy-start | bytes 1572868
  24.3 8.1 %copy-start.3 = (f32[23,1,2048]{2,0,1:T(8,128)S(1)}, f32[23,1,2048]{2,0,1:T(8,128)}, u32[]{:S(2)}) copy-start(f32[23,1,2048]{2,0,1:T(8,128)} %copy-done.2) | copy-start | bytes 565252
  242.7 10.0 %copy-start = (f32[120,10,2048]{2,1,0:T(8,128)S(1)}, f32[120,10,2048]{2,1,0:T(8,128)}, u32[]{:S(2)}) copy-start(f32[120,10,2048]{2,1,0:T(8,128)} %broadcast_select_fusion.1) | copy-start | bytes 29491204
Sparse Core Ops, SparseCore 0:
  18.9 182.0 all-gather.1
where the time goes:
time: 302 us
  waiting for transfers between devices  170 us (56%)
  local copies, waits for them, and re-layouts  61.7 us (20%)
  other arithmetic  53.2 us (18%)
  between operations  13.7 us (5%)
    all_gather x1, waiting for transfers between devices, local(): every = lax.all_gather(source, 'chaos', axis=0, tiled=True)  166 us
    reduce_sum x1, other arithmetic, local(): return 0.5 * jnp.sum(result, axis=0)  18.3 us
    slice x2, local copies, waits for them, and re-layouts, shift_cols(): return jnp.concatenate([zero, x[..., :-1]], axis=-1)  15.9 us
    gather x1, local copies, waits for them, and re-layouts, local(): jnp.take(every, last.reshape(-1), axis=0)  15 us
    gather x1, local copies, waits for them, and re-layouts, local(): jnp.take(every, first.reshape(-1), axis=0)  15 us
    select_n x2, other arithmetic, local(): jnp.take(every, first.reshape(-1), axis=0)  11.6 us
    add x1, other arithmetic, local(): w_first[:, :, None, None] * g_first + w_last[:, :, None, None] * g_last  7.05 us
    select_n x2, other arithmetic, local(): jnp.take(every, last.reshape(-1), axis=0)  6.84 us
  transfers between devices with their start and end apart: 3, of which 2 were waited for; matrix products, arithmetic and copies ran while one was open for 5% of the time, Pallas kernels for 0%

commit v1 on v0

--- a/solution.py
+++ b/solution.py
@@ -2,6 +2,11 @@
 import jax.numpy as jnp
 from jax import lax
 from jax.sharding import PartitionSpec as P
+
+
+def gather_over(x, axis, dim):
+    repeated = jnp.stack([x] * lax.axis_size(axis))
+    return jnp.concatenate(lax.all_to_all(repeated, axis, 0, 0), axis=dim)
 
 
 def extended_2(x, sides, width):
@@ -59,7 +64,7 @@
     padded = extended_2(joined, (("space", 1),), 1)
     source = padded[:own_modes]
     coef = padded[own_modes:]
-    every = lax.all_gather(source, "chaos", axis=0, tiled=True)
+    every = gather_over(source, "chaos", 0)
     a_c = coef[:, 1:-1]
     c_up = (a_c + coef[:, :-2])[:, None]
     c_dn = (a_c + coef[:, 2:])[:, None]

time: 302 us -> 273 us (0.904); the launches traced: 302 us -> 269 us
  waiting for transfers between devices: 170 us -> 132 us
  between operations: 13.7 us -> 0.28 us
  local copies, waits for them, and re-layouts: 61.7 us -> 69.2 us
  starting transfers between devices: 2.63 us -> 9.67 us
  other arithmetic: 53.2 us -> 57.5 us
    all_gather x1 -> x0, waiting for transfers between devices: 166 us -> none  [local(): every = lax.all_gather(source, 'chaos', axis=0, tiled=True)]
    all_to_all x0 -> x1, waiting for transfers between devices: none -> 128 us  [gather_over(): return jnp.concatenate(lax.all_to_all(repeated, axis, 0, 0), axis=dim)]
    reshape x0 -> x1, local copies, waits for them, and re-layouts: none -> 16 us  [gather_over(): return jnp.concatenate(lax.all_to_all(repeated, axis, 0, 0), axis=dim)]
    add x1, other arithmetic: 7.05 us -> 19 us  [local(): w_first[:, :, None, None] * g_first + w_last[:, :, None, None] * g_last]
    slice x2, local copies, waits for them, and re-layouts: 15.9 us -> 5.68 us  [shift_cols(): return jnp.concatenate([zero, x[..., :-1]], axis=-1)]
    reduce_sum x1, other arithmetic: 18.3 us -> 8.79 us  [local(): return 0.5 * jnp.sum(result, axis=0)]
    all_to_all x0 -> x1, starting transfers between devices: none -> 7.07 us  [gather_over(): return jnp.concatenate(lax.all_to_all(repeated, axis, 0, 0), axis=dim)]
    another operation x0 -> x1, local copies, waits for them, and re-layouts: none -> 5.31 us  [gather_over(): repeated = jnp.stack([x] * lax.axis_size(axis))]
  transfers between devices with their start and end apart: 3 -> 3, of which waited for: 2 -> 2; matrix products, arithmetic and copies ran while one was open for 5% -> 6% of each run, Pallas kernels for 0% -> 0%
where the time goes in v1:
time: 273 us; the launch traced here: 269 us
  waiting for transfers between devices  132 us (48%)
  local copies, waits for them, and re-layouts  69.2 us (25%)
  other arithmetic  57.5 us (21%)
  starting transfers between devices  9.67 us (4%)
    all_to_all x1, waiting for transfers between devices, gather_over(): return jnp.concatenate(lax.all_to_all(repeated, axis, 0, 0), axis=dim)  128 us
    add x1, other arithmetic, local(): w_first[:, :, None, None] * g_first + w_last[:, :, None, None] * g_last  19 us
    reshape x1, local copies, waits for them, and re-layouts, gather_over(): return jnp.concatenate(lax.all_to_all(repeated, axis, 0, 0), axis=dim)  16 us
    gather x1, local copies, waits for them, and re-layouts, local(): jnp.take(every, last.reshape(-1), axis=0)  15.3 us
    gather x1, local copies, waits for them, and re-layouts, local(): jnp.take(every, first.reshape(-1), axis=0)  15 us
    select_n x2, other arithmetic, local(): jnp.take(every, first.reshape(-1), axis=0)  12.8 us
    reduce_sum x1, other arithmetic, local(): return 0.5 * jnp.sum(result, axis=0)  8.79 us
    all_to_all x1, starting transfers between devices, gather_over(): return jnp.concatenate(lax.all_to_all(repeated, axis, 0, 0), axis=dim)  7.07 us
  transfers between devices with their start and end apart: 3, of which 2 were waited for; matrix products, arithmetic and copies ran while one was open for 6% of the time, Pallas kernels for 0%

profile of v1, /device:TPU:0, one launch (start us, length us, event | category | flops | bytes accessed | tf_op | source)
XLA Modules:
  0.0 268.6 jit_solution(9394252604316788404)
XLA Ops:
  0.0 1.8 copy.60
  1.8 1.4 copy.62
  3.2 1.3 collective-permute-start
  4.5 1.3 collective-permute-start.1
  5.8 4.3 %collective-permute-done.1 = f32[23,1,2048]{2,0,1:T(8,128)S(1)} collective-permute-done((f32[23,1,2048]{2,0,1:T(8,128)S(1)}, f32[23,1,2048]{2,0,1:T(8,128)S(1)}, u32[]{:S(2)}, u32[]{:S(2)}) %collective-permute-start.1) | collective-permute-done | bytes 188448 | tf_op jit(solution)/shard_map/ppermute | solution.py:20
  10.1 0.1 pad_maximum_fusion
  10.2 5.3 %stack.2 = f32[8,15,10,2048]{3,1,2,0:T(8,128)} broadcast(f32[15,10,2048]{2,0,1:T(8,128)S(1)} %pad_maximum_fusion), dimensions={1,2,3} | broadcast | bytes 11059200 | tf_op jit(solution)/shard_map/stack | solution.py:8
  15.5 7.1 %all-to-all-start = ((f32[8,15,10,2048]{3,1,2,0:T(8,128)}), f32[8,15,10,2048]{3,1,2,0:T(8,128)}, u32[]{:S(2)}, u32[]{:S(2)}) async-start(f32[8,15,10,2048]{3,1,2,0:T(8,128)} %stack.2), calls=%async_computation | async-start | bytes 20971520 | tf_op jit(solution)/shard_map/all_to_all | solution.py:9
  22.6 0.1 select_reduce_fusion
  22.9 4.7 %scatter_custom_fusion = f32[115200]{0:T(1024)S(1)} fusion(s32[624]{0:T(1024)S(1)} %fusion.23, f32[624]{0:T(1024)S(1)} %fusion.25, f32[]{:T(128)} %constant.6.clone.1), kind=kCustom, calls=%fused_computation.31 | custom fusion | flops 624 | bytes 460804 | tf_op jit(solution)/shard_map/scatter-add | solution.py:38
  27.6 0.5 reshape.52
  28.1 0.1 rev.3
  28.2 1.1 iota_reduce_fusion.1
  29.4 0.9 iota_reduce_fusion
  30.5 2.1 gather_fusion.2
  32.7 2.1 gather_fusion
  34.9 0.2 fusion.27
  35.1 0.2 pad_add_fusion.1
  35.4 0.3 copy.69
  35.7 0.3 copy.70
  36.1 1.8 fusion.8
  37.9 127.8 %all-to-all-done = f32[8,15,10,2048]{3,1,2,0:T(8,128)} async-done(((f32[8,15,10,2048]{3,1,2,0:T(8,128)}), f32[8,15,10,2048]{3,1,2,0:T(8,128)}, u32[]{:S(2)}, u32[]{:S(2)}) %all-to-all-start) | async-done | bytes 9830432 | tf_op jit(solution)/shard_map/all_to_all | solution.py:9
  165.7 16.0 %copy.72 = f32[8,15,10,2048]{3,2,1,0:T(8,128)} copy(f32[8,15,10,2048]{3,1,2,0:T(8,128)} %all-to-all-done) | data formatting | bytes 19660800 | tf_op jit(solution)/shard_map/reshape | solution.py:9
  181.7 15.0 %gather_fusion.1 = f32[120,10,2048]{2,1,0:T(8,128)} fusion(f32[120,10,2048]{2,1,0:T(8,128)} %bitcast.31, s32[1024]{0:T(1024)S(1)} %pad_clamp_fusion.1), kind=kCustom, calls=%fused_computation.1.clone | custom fusion | bytes 19661280 | tf_op jit(solution)/shard_map/jit(_take)/gather | solution.py:73
  196.7 15.3 %gather_fusion.3 = f32[120,10,2048]{2,1,0:T(8,128)} fusion(f32[120,10,2048]{2,1,0:T(8,128)} %bitcast.32, s32[1024]{0:T(1024)S(1)} %pad_clamp_fusion), kind=kCustom, calls=%fused_computation.3.clone | custom fusion | bytes 19661280 | tf_op jit(solution)/shard_map/jit(_take)/gather | solution.py:76
  212.0 12.8 %broadcast_select_fusion.1 = f32[120,10,2048]{2,1,0:T(8,128)} fusion(f32[120,10,2048]{2,1,0:T(8,128)} %gather_fusion.1, pred[120]{0:T(512)(128)(4,1)S(1)} %compare_and_fusion.1), kind=kLoop, calls=%fused_computation.17 | loop fusion | flops 2457600 | bytes 19660920 | tf_op jit(solution)/shard_map/jit(_take)/select_n | solution.py:73
  224.8 2.9 %copy-done = f32[120,10,2048]{2,1,0:T(8,128)S(1)} copy-done((f32[120,10,2048]{2,1,0:T(8,128)S(1)}, f32[120,10,2048]{2,1,0:T(8,128)}, u32[]{:S(2)}) %copy-start) | copy-done | bytes 9830424
  227.7 6.1 %broadcast_select_fusion = f32[120,10,2048]{2,1,0:T(8,128)} fusion(f32[120,10,2048]{2,1,0:T(8,128)S(1)} %copy-done, pred[120]{0:T(512)(128)(4,1)S(1)} %compare_and_fusion), kind=kLoop, calls=%fused_computation.16 | loop fusion | flops 2457600 | bytes 19660920 | tf_op jit(solution)/shard_map/jit(_take)/select_n | solution.py:76
  233.8 19.0 %fusion = f32[8,15,10,2048]{3,1,0,2:T(8,128)S(1)} fusion(f32[8,15,10,2048]{3,2,1,0:T(8,128)} %bitcast.34, f32[8,15,10,2048]{3,2,1,0:T(8,128)} %bitcast.33, f32[8,15]{1,0:T(8,128)S(1)} %bitcast_select_fusion, f32[8,15]{1,0:T(8,128)S(1)} %select_bitcast_fusion), kind=kLoop, calls=%fused_computation.6 | loop fusion | flops 7372800 | bytes 29492160 | tf_op jit(solution)/shard_map/add | solution.py:79
  252.8 5.5 %fusion.26 = (f32[8,15,8,2047]{3,1,0,2:T(8,128)S(1)}, f32[8,15,8,2047]{3,1,0,2:T(8,128)}) fusion(f32[8,15,10,2048]{3,1,0,2:T(8,128)S(1)} %fusion), kind=kLoop, calls=%fused_computation.78 | loop fusion | bytes 31441920 | tf_op jit(solution)/shard_map/slice | solution.py:28
  258.3 8.8 %fusion.5 = f32[15,8,2048]{2,0,1:T(8,128)S(1)} fusion(f32[8,15,10,2048]{3,1,0,2:T(8,128)S(1)} %fusion, f32[8,15,8,2047]{3,1,0,2:T(8,128)} %get-tuple-element.14, f32[8,15,8,2047]{3,1,0,2:T(8,128)S(1)} %get-tuple-element.13, f32[8,8,2048]{2,0,1:T(8,128)S(1)} %copy.70, f32[8,8,2048]{2,0,1:T(8,128)S(1)} %copy.69, f32[8,8,2048]{2,0,1:T(8,128)S(1)} %copy-done.2, ...), kind=kLoop, calls=%fused_computation.13 | loop fusion | flops 23347200 | bytes 42394112 | tf_op jit(solution)/shard_map/reduce_sum | solution.py:85
  267.1 1.6 copy_multiply_fusion.2
  (41 shorter events, 0.7 us)
Async XLA Ops:
  3.2 2.6 collective-permute-start
  4.5 5.6 %collective-permute-start.1 = (f32[23,1,2048]{2,0,1:T(8,128)S(1)}, f32[23,1,2048]{2,0,1:T(8,128)S(1)}, u32[]{:S(2)}, u32[]{:S(2)}) collective-permute-start(f32[23,1,2048]{2,0,1:T(8,128)S(1)} %get-tuple-element.18), channel_id=1, source_target_pairs={{1,0},{2,1},{3,2},{4,3},{5,4},{6,5},{7,6},{8,7},{9,8},{10,9},{11,1... | collective-permute-start | bytes 565256 | tf_op jit(solution)/shard_map/ppermute | solution.py:20
  10.1 5.4 %copy-start.3 = (f32[23,1,2048]{2,0,1:T(8,128)}, f32[23,1,2048]{2,0,1:T(8,128)S(1)}, u32[]{:S(2)}) copy-start(f32[23,1,2048]{2,0,1:T(8,128)S(1)} %collective-permute-done.1) | copy-start | bytes 565252
  15.5 7.1 %slice-start = ((s32[624,3]{0,1:T(4,128)}), s32[624,2]{0,1:T(2,128)S(1)}, s32[]{:S(2)}) async-start(s32[624,3]{0,1:T(4,128)} %param.11), calls=%async_computation.1 | async-start | bytes 10240 | tf_op jit(solution)/shard_map/slice | solution.py:33
  15.5 7.1 %copy-start.6 = (s32[120]{0:T(128)S(1)}, s32[120]{0:T(128)}, u32[]{:S(2)}) copy-start(s32[120]{0:T(128)} %param.13) | copy-start | bytes 1444
  15.5 7.3 %copy-start.4 = (s32[624,3]{0,1:T(4,128)S(1)}, s32[624,3]{0,1:T(4,128)}, u32[]{:S(2)}) copy-start(s32[624,3]{0,1:T(4,128)} %param.11) | copy-start | bytes 22468
  15.5 7.3 %copy-start.5 = (s32[624,2]{0,1:T(2,128)S(1)}, s32[624,2]{0,1:T(2,128)}, u32[]{:S(2)}) copy-start(s32[624,2]{0,1:T(2,128)} %param.12) | copy-start | bytes 14980
  15.5 150.2 %all-to-all-start = ((f32[8,15,10,2048]{3,1,2,0:T(8,128)}), f32[8,15,10,2048]{3,1,2,0:T(8,128)}, u32[]{:S(2)}, u32[]{:S(2)}) async-start(f32[8,15,10,2048]{3,1,2,0:T(8,128)} %stack.2), calls=%async_computation | async-start | bytes 20971520 | tf_op jit(solution)/shard_map/all_to_all | solution.py:9
  22.6 12.3 %copy-start.1 = (f32[8,8,2048]{2,1,0:T(8,128)S(1)}, f32[8,8,2048]{2,1,0:T(8,128)}, u32[]{:S(2)}) copy-start(f32[8,8,2048]{2,1,0:T(8,128)} %param.10) | copy-start | bytes 1572868
  212.0 15.7 %copy-start = (f32[120,10,2048]{2,1,0:T(8,128)S(1)}, f32[120,10,2048]{2,1,0:T(8,128)}, u32[]{:S(2)}) copy-start(f32[120,10,2048]{2,1,0:T(8,128)} %gather_fusion.3) | copy-start | bytes 29491204
  252.8 5.5 %copy-start.2 = (f32[8,8,2048]{2,0,1:T(8,128)S(1)}, f32[8,8,2048]{2,0,1:T(8,128)}, u32[]{:S(2)}) copy-start(f32[8,8,2048]{2,0,1:T(8,128)} %get-tuple-element.16) | copy-start | bytes 1572868
